TPU v7x, 32 devices: a whole 2x2x4 slice. The times are simulated.
32 devices in a mesh: grp: 4 (over x, core), ep: 8 (over z, y).
Axes of the slice: x: 2, y: 2, z: 4, core: 2. Of those that a mesh axis runs over, the one named last changes fastest.
Arguments:
- tokens: bfloat16 [2048, 5120], P('ep', 'grp'), may hold values from -6 to 6
- cotangent: bfloat16 [2048, 5120], P('ep', 'grp'), may hold values from -0.59765625 to 0.59765625
- gate_weights: bfloat16 [2048, 6], P('ep'), may hold values from 0.099609375 to 1
- expert_ids: int32 [2048, 6], P('ep'), may hold values from 0 to 159, all different within a row; in each aligned block of 256 rows (0 to 255, 256 to 511, ...) at most 16 rows name the same one
- hot_ids: int32 [2], replicated, may hold values from 8 to 159, as said below
- gate_cold: bfloat16 [8, 5120, 768], P('ep', 'grp'), may hold values from -0.078125 to 0.078125
- up_cold: bfloat16 [8, 5120, 768], P('ep', 'grp'), may hold values from -0.078125 to 0.078125
- down_cold: bfloat16 [8, 768, 5120], P('ep', None, 'grp'), may hold values from -0.21875 to 0.21875
- gate_hot: bfloat16 [2, 5120, 768], P(None, 'grp', 'ep'), may hold values from -0.078125 to 0.078125
- up_hot: bfloat16 [2, 5120, 768], P(None, 'grp', 'ep'), may hold values from -0.078125 to 0.078125
- down_hot: bfloat16 [2, 768, 5120], P(None, 'ep', 'grp'), may hold values from -0.21875 to 0.21875
Outputs:
- grad_gate_cold: bfloat16 [8, 5120, 768], P('ep', 'grp')
- grad_up_cold: bfloat16 [8, 5120, 768], P('ep', 'grp')
- grad_down_cold: bfloat16 [8, 768, 5120], P('ep', None, 'grp')
- grad_gate_hot: float32 [2, 5120, 768], P(None, 'grp', 'ep')
- grad_up_hot: float32 [2, 5120, 768], P(None, 'grp', 'ep')
- grad_down_hot: float32 [2, 768, 5120], P(None, 'ep', 'grp')
- gate_weight_grad: float32 [2048, 6], P('ep')
Inputs may be any that keep to these rules, and one draw needn't show every extreme that they name: `expert_ids`: each row names 6 different experts. Among the routes of the 256 tokens of one index of ep (aligned blocks of rows) no expert is named more than 16 times, a bound that some block reaches. `hot_ids`: distinct expert numbers, none below 8; expert 160 - 1 is always among them.
All inputs are finite; a program needn't handle non-finite values.
Results may differ from a plain program's by a relative error of at most 0.02.
Values may be sent and summed in bfloat16 or wider, within the bound.
No kernel may reach another device: no remote copies, remote signals or barrier semaphores. Data moves between devices by JAX's collectives and lax.ppermute only.
A program may use at most 128 MiB of HBM per device.

v0:
```python
import jax
import jax.numpy as jnp
from jax import lax
from jax.sharding import PartitionSpec as P


def route_table(flat_ids, targets, capacity):
    matches = (flat_ids[:, None] == targets[None, :]).astype(jnp.int32)
    rank_of = jnp.cumsum(matches, axis=0) - 1
    slot_of = jnp.sum(matches * rank_of, axis=1)
    owner_of = jnp.sum(matches * jnp.arange(targets.shape[0], dtype=jnp.int32)[None, :], axis=1)
    usable = jnp.sum(matches, axis=1) > 0
    row_of = owner_of * capacity + slot_of
    rows_total = targets.shape[0] * capacity
    route_map = (row_of[None, :] == jnp.arange(rows_total, dtype=jnp.int32)[:, None]) & usable[
        None, :
    ]
    return route_map.astype(jnp.float32)


def gather_rows(route_map, tokens, cotangent, flat_weights, tok_rows, top_count):
    per_token = jnp.sum(route_map.reshape(route_map.shape[0], tok_rows, top_count), axis=2)
    token_map = per_token.astype(jnp.bfloat16)
    feat_rows = jnp.dot(token_map, tokens, preferred_element_type=jnp.float32).astype(jnp.bfloat16)
    cotan_rows = jnp.dot(token_map, cotangent, preferred_element_type=jnp.float32).astype(
        jnp.bfloat16
    )
    scale_rows = jnp.dot(
        route_map, flat_weights.astype(jnp.float32), precision=lax.Precision.HIGHEST
    )
    return (feat_rows, cotan_rows, scale_rows.astype(jnp.bfloat16))


def swiglu_back(pre_gate, pre_up, grad_hidden):
    sigmoid_gate = jax.nn.sigmoid(pre_gate)
    activated = pre_gate * sigmoid_gate
    hidden = (activated * pre_up).astype(jnp.bfloat16)
    back_gate = (
        grad_hidden * pre_up * sigmoid_gate * (1.0 + pre_gate * (1.0 - sigmoid_gate))
    ).astype(jnp.bfloat16)
    back_up = (grad_hidden * activated).astype(jnp.bfloat16)
    return (hidden, back_gate, back_up)


def body(
    tokens,
    cotangent,
    gate_weights,
    expert_ids,
    hot_ids,
    gate_cold,
    up_cold,
    down_cold,
    gate_hot,
    up_hot,
    down_hot,
):
    tok_rows, slice_width = tokens.shape
    top_count = expert_ids.shape[1]
    cold_count = lax.axis_size("ep")
    hot_count = hot_ids.shape[0]
    capacity = tok_rows // 16
    flat_ids = expert_ids.reshape(-1)
    flat_weights = gate_weights.reshape(-1)
    cold_map = route_table(flat_ids, jnp.arange(cold_count, dtype=jnp.int32), capacity)
    hot_map = route_table(flat_ids, hot_ids, capacity)
    cold_feats, cold_cotan, cold_scale = gather_rows(
        cold_map, tokens, cotangent, flat_weights, tok_rows, top_count
    )
    hot_feats, hot_cotan, hot_scale = gather_rows(
        hot_map, tokens, cotangent, flat_weights, tok_rows, top_count
    )
    outgoing = (
        cold_feats.reshape(cold_count, capacity, slice_width),
        cold_cotan.reshape(cold_count, capacity, slice_width),
        cold_scale.reshape(cold_count, capacity),
    )
    recv_feats, recv_cotan, recv_scale = (
        lax.all_to_all(outgoing[0], "ep", split_axis=0, concat_axis=0, tiled=True),
        lax.all_to_all(outgoing[1], "ep", split_axis=0, concat_axis=0, tiled=True),
        lax.all_to_all(outgoing[2], "ep", split_axis=0, concat_axis=0, tiled=True),
    )
    recv_feats = recv_feats.reshape(-1, slice_width)
    recv_cotan = recv_cotan.reshape(-1, slice_width)
    weighted = (
        recv_scale.reshape(-1).astype(jnp.float32)[:, None] * recv_cotan.astype(jnp.float32)
    ).astype(jnp.bfloat16)
    w_gate = gate_cold[0]
    w_up = up_cold[0]
    w_down = down_cold[0]
    part_gate = jnp.dot(recv_feats, w_gate, preferred_element_type=jnp.float32)
    part_up = jnp.dot(recv_feats, w_up, preferred_element_type=jnp.float32)
    part_hidden = lax.dot_general(
        weighted, w_down, (((1,), (1,)), ((), ())), preferred_element_type=jnp.float32
    )
    pre_gate, pre_up, grad_hidden = (
        lax.psum(part_gate.astype(jnp.bfloat16), "grp").astype(jnp.float32),
        lax.psum(part_up.astype(jnp.bfloat16), "grp").astype(jnp.float32),
        lax.psum(part_hidden.astype(jnp.bfloat16), "grp").astype(jnp.float32),
    )
    hidden, back_gate, back_up = swiglu_back(pre_gate, pre_up, grad_hidden)
    output_slice = jnp.dot(hidden, w_down, preferred_element_type=jnp.float32)
    cold_route = jnp.sum(output_slice * recv_cotan.astype(jnp.float32), axis=1)
    contract_rows = (((0,), (0,)), ((), ()))
    grad_gate_cold = lax.dot_general(
        recv_feats, back_gate, contract_rows, preferred_element_type=jnp.float32
    )
    grad_up_cold = lax.dot_general(
        recv_feats, back_up, contract_rows, preferred_element_type=jnp.float32
    )
    grad_down_cold = lax.dot_general(
        hidden, weighted, contract_rows, preferred_element_type=jnp.float32
    )
    hot_weighted_local = (
        hot_scale.astype(jnp.float32)[:, None] * hot_cotan.astype(jnp.float32)
    ).astype(jnp.bfloat16)
    blocks = lax.axis_size("ep")
    stacked = jnp.stack([hot_feats, hot_cotan, hot_weighted_local])
    all_rows = lax.all_gather(stacked, "ep", axis=1, tiled=False)
    all_rows = all_rows.reshape(3, blocks, hot_count, capacity, slice_width)
    all_rows = jnp.transpose(all_rows, (0, 2, 1, 3, 4)).reshape(
        3, hot_count, blocks * capacity, slice_width
    )
    rows_feat, rows_cot, rows_wt = (all_rows[0], all_rows[1], all_rows[2])
    part_gate_hot = jnp.einsum(
        "jrd,jdh->jrh", rows_feat, gate_hot, preferred_element_type=jnp.float32
    )
    part_up_hot = jnp.einsum("jrd,jdh->jrh", rows_feat, up_hot, preferred_element_type=jnp.float32)
    part_hidden_hot = jnp.einsum(
        "jrd,jhd->jrh", rows_wt, down_hot, preferred_element_type=jnp.float32
    )
    cot_down = jnp.einsum("jrd,jhd->jrh", rows_cot, down_hot, preferred_element_type=jnp.float32)
    hot_parts = lax.psum(
        jnp.stack([part_gate_hot, part_up_hot, part_hidden_hot]).astype(jnp.bfloat16), "grp"
    ).astype(jnp.float32)
    hidden_hot, back_gate_hot, back_up_hot = swiglu_back(hot_parts[0], hot_parts[1], hot_parts[2])
    hot_route_part = jnp.sum(hidden_hot.astype(jnp.float32) * cot_down, axis=2)
    hidden_blk = hidden_hot.shape[2]
    feat_b = rows_feat.reshape(hot_count, blocks, capacity, slice_width)
    wt_b = rows_wt.reshape(hot_count, blocks, capacity, slice_width)
    bg_b = back_gate_hot.reshape(hot_count, blocks, capacity, hidden_blk)
    bu_b = back_up_hot.reshape(hot_count, blocks, capacity, hidden_blk)
    hid_b = hidden_hot.reshape(hot_count, blocks, capacity, hidden_blk)
    blk_gate = jnp.einsum("jbcd,jbch->jbdh", feat_b, bg_b, preferred_element_type=jnp.float32)
    blk_up = jnp.einsum("jbcd,jbch->jbdh", feat_b, bu_b, preferred_element_type=jnp.float32)
    blk_down = jnp.einsum("jbch,jbcd->jbhd", hid_b, wt_b, preferred_element_type=jnp.float32)
    grad_gate_hot = jnp.sum(blk_gate.astype(jnp.bfloat16).astype(jnp.float32), axis=1)
    grad_up_hot = jnp.sum(blk_up.astype(jnp.bfloat16).astype(jnp.float32), axis=1)
    grad_down_hot = jnp.sum(blk_down.astype(jnp.bfloat16).astype(jnp.float32), axis=1)
    hot_route_all = lax.psum(hot_route_part, ("grp", "ep"))
    me = lax.axis_index("ep")
    hot_route = lax.dynamic_index_in_dim(
        hot_route_all.reshape(hot_count, blocks, capacity), me, axis=1, keepdims=False
    )
    cold_route = lax.psum(cold_route, "grp")
    cold_back = lax.all_to_all(
        cold_route.reshape(cold_count, capacity), "ep", split_axis=0, concat_axis=0, tiled=True
    )
    route_flat = jnp.dot(cold_back.reshape(-1), cold_map, precision=lax.Precision.HIGHEST)
    route_flat = route_flat + jnp.dot(
        hot_route.reshape(-1), hot_map, precision=lax.Precision.HIGHEST
    )
    gate_weight_grad = route_flat.reshape(tok_rows, top_count)
    return (
        grad_gate_cold[None].astype(jnp.bfloat16),
        grad_up_cold[None].astype(jnp.bfloat16),
        grad_down_cold[None].astype(jnp.bfloat16),
        grad_gate_hot,
        grad_up_hot,
        grad_down_hot,
        gate_weight_grad,
    )


def solution(mesh):
    in_specs = (
        P("ep", "grp"),
        P("ep", "grp"),
        P("ep", None),
        P("ep", None),
        P(),
        P("ep", "grp", None),
        P("ep", "grp", None),
        P("ep", None, "grp"),
        P(None, "grp", "ep"),
        P(None, "grp", "ep"),
        P(None, "ep", "grp"),
    )
    out_specs = (
        P("ep", "grp", None),
        P("ep", "grp", None),
        P("ep", None, "grp"),
        P(None, "grp", "ep"),
        P(None, "grp", "ep"),
        P(None, "ep", "grp"),
        P("ep", None),
    )
    return jax.shard_map(body, mesh=mesh, in_specs=in_specs, out_specs=out_specs, check_vma=False)
```

profile of v0, /device:TPU:0, one launch (start us, length us, event | category | flops | bytes accessed | tf_op | source)
XLA Modules:
  0.0 194.5 jit_solution(9976301442183095189)
XLA Ops:
  12.8 1.3 convolution_convert_fusion.8
  15.2 2.3 %reduce-window.14 = s32[8,12,128]{2,1,0:T(8,128)S(1)} reduce-window(s32[8,12,128]{2,1,0:T(8,128)S(1)} %fusion.69, s32[]{:T(128)} %constant.15.clone.1), window={size=1x1x128 pad=0_0x0_0x127_0}, to_apply=%region_1.2 | reduce-window | flops 1560576 | bytes 98308 | tf_op jit(solution)/shard_map/reduce-window
  19.1 7.3 %all-to-all-start.1 = ((bf16[8,1,16]{2,1,0:T(2,128)(2,1)}), bf16[8,1,16]{2,1,0:T(2,128)(2,1)S(1)}, u32[]{:S(2)}, u32[]{:S(2)}) async-start(bf16[8,1,16]{2,1,0:T(2,128)(2,1)} %all_to_all.24), calls=%async_computation.1 | async-start | bytes 8192 | tf_op jit(solution)/shard_map/all_to_all | solution.py:81
  28.0 4.8 %all-to-all-done.1 = bf16[8,1,16]{2,1,0:T(2,128)(2,1)S(1)} async-done(((bf16[8,1,16]{2,1,0:T(2,128)(2,1)}), bf16[8,1,16]{2,1,0:T(2,128)(2,1)S(1)}, u32[]{:S(2)}, u32[]{:S(2)}) %all-to-all-start.1) | async-done | bytes 288 | tf_op jit(solution)/shard_map/all_to_all | solution.py:81
  32.8 3.4 %all-to-all-start = ((bf16[8,16,1280]{2,1,0:T(8,128)(2,1)}), bf16[8,16,1280]{2,1,0:T(8,128)(2,1)S(1)}, u32[]{:S(2)}, u32[]{:S(2)}) async-start(bf16[8,16,1280]{2,1,0:T(8,128)(2,1)} %bitcast.165), calls=%async_computation | async-start | bytes 655360 | tf_op jit(solution)/shard_map/all_to_all | solution.py:79
  37.3 9.1 %all-to-all-done = bf16[8,16,1280]{2,1,0:T(8,128)(2,1)S(1)} async-done(((bf16[8,16,1280]{2,1,0:T(8,128)(2,1)}), bf16[8,16,1280]{2,1,0:T(8,128)(2,1)S(1)}, u32[]{:S(2)}, u32[]{:S(2)}) %all-to-all-start) | async-done | bytes 327712 | tf_op jit(solution)/shard_map/all_to_all | solution.py:79
  46.4 3.9 %all-to-all-start.2 = ((bf16[8,16,1280]{2,1,0:T(8,128)(2,1)}), bf16[8,16,1280]{2,1,0:T(8,128)(2,1)S(1)}, u32[]{:S(2)}, u32[]{:S(2)}) async-start(bf16[8,16,1280]{2,1,0:T(8,128)(2,1)} %bitcast.166), calls=%async_computation.2 | async-start | bytes 655360 | tf_op jit(solution)/shard_map/all_to_all | solution.py:80
  50.3 2.8 %fusion.20 = bf16[128,768]{1,0:T(8,128)(2,1)} fusion(bf16[128,1280]{1,0:T(8,128)(2,1)S(1)} %bitcast.155, bf16[1,1280,768]{2,1,0:T(8,128)(2,1)} %param.16), kind=kOutput, calls=%fused_computation.29 | convolution fusion | flops 251756544 | bytes 2490368 | tf_op jit(solution)/shard_map/dot_general | solution.py:91
  54.3 14.6 %all-to-all-done.2 = bf16[8,16,1280]{2,1,0:T(8,128)(2,1)S(1)} async-done(((bf16[8,16,1280]{2,1,0:T(8,128)(2,1)}), bf16[8,16,1280]{2,1,0:T(8,128)(2,1)S(1)}, u32[]{:S(2)}, u32[]{:S(2)}) %all-to-all-start.2) | async-done | bytes 327712 | tf_op jit(solution)/shard_map/all_to_all | solution.py:80
  69.0 1.5 fusion.14
  70.5 2.1 %all-gather.3.cloned.1.call-done = bf16[3,256,1280]{2,1,0:T(8,128)(2,1)} async-done(((bf16[3,32,1280]{2,1,0:T(8,128)(2,1)}), bf16[3,256,1280]{2,1,0:T(8,128)(2,1)}) %all-gather.3.cloned.1.call-update) | async-done | bytes 1966096 | tf_op jit(solution)/shard_map/all_gather | solution.py:119
  72.6 1.7 copy.68
  78.1 33.6 %all-reduce.3.cloned.1.call-done = (bf16[128,768]{1,0:T(8,128)(2,1)}, bf16[128,768]{1,0:T(8,128)(2,1)}, bf16[128,768]{1,0:T(8,128)(2,1)}, bf16[3,2,128,96]{2,3,1,0:T(8,128)(2,1)}) async-done(((bf16[128,768]{1,0:T(8,128)(2,1)}, bf16[128,768]{1,0:T(8,128)(2,1)}, bf16[128,768]{1,0:T(8,128)(2,1)}, bf16[3,2,128,96]{2,3,1,0:T(8,128)(2,1)}), (bf16[128,768]{1,0:T(8,128)(2,1)}, bf16[128,768]{1,0:T(8,128)(2,1)}, ...) | async-done | bytes 737296 | tf_op jit(solution)/shard_map/psum | solution.py:98
  111.7 1.6 convert_element_type.217
  114.5 3.3 %convert_reduce_fusion = f32[2,96,1280]{2,1,0:T(8,128)} fusion(f32[2,8,16,96]{3,2,1,0:T(8,128)S(1)} %bitcast.169, f32[2,8,16,96]{3,2,1,0:T(8,128)S(1)} %bitcast.171, bf16[3,2,8,16,1280]{4,3,2,1,0:T(8,128)(2,1)} %bitcast.152), kind=kOutput, calls=%fused_computation | convolution fusion | flops 68714496 | bytes 1835008 | tf_op jit(solution)/shard_map/jbch,jbcd->jbhd/dot_general | solution.py:146
  117.8 3.3 %convert_reduce_fusion.2 = f32[2,1280,96]{1,2,0:T(8,128)} fusion(f32[2,8,16,96]{3,2,1,0:T(8,128)S(1)} %bitcast.172, f32[2,8,16,96]{3,2,1,0:T(8,128)S(1)} %bitcast.174, f32[2,8,16,96]{3,2,1,0:T(8,128)S(1)} %bitcast.170, bf16[3,2,8,16,1280]{4,3,2,1,0:T(8,128)(2,1)} %bitcast.153), kind=kOutput, calls=%fused_computation.2 | convolution fusion | flops 68812800 | bytes 1933312 | tf_op jit(solution)/shard_map/jbcd,jbch->jbdh/dot_general | solution.py:144
  121.1 3.4 %convert_reduce_fusion.1 = f32[2,1280,96]{1,2,0:T(8,128)} fusion(f32[2,8,16,96]{3,2,1,0:T(8,128)S(1)} %bitcast.175, f32[2,8,16,96]{3,2,1,0:T(8,128)S(1)} %bitcast.173, bf16[3,2,8,16,1280]{4,3,2,1,0:T(8,128)(2,1)} %bitcast.154), kind=kOutput, calls=%fused_computation.1 | convolution fusion | flops 68714496 | bytes 1835008 | tf_op jit(solution)/shard_map/jbcd,jbch->jbdh/dot_general | solution.py:145
  124.6 2.0 %fusion.1 = bf16[1,1280,768]{2,1,0:T(8,128)(2,1)} fusion(bf16[128,1280]{1,0:T(8,128)(2,1)S(1)} %bitcast.157, bf16[128,768]{1,0:T(8,128)(2,1)S(1)} %copy-done.7, bf16[128,768]{1,0:T(8,128)(2,1)S(1)} %copy-done.5), kind=kOutput, calls=%fused_computation.10 | convolution fusion | flops 253427712 | bytes 2686976 | tf_op jit(solution)/shard_map/dot_general | solution.py:108
  126.5 2.0 %fusion = bf16[1,1280,768]{2,1,0:T(8,128)(2,1)} fusion(bf16[128,1280]{1,0:T(8,128)(2,1)S(1)} %bitcast.158, bf16[128,768]{1,0:T(8,128)(2,1)S(1)} %copy-done.6, bf16[128,768]{1,0:T(8,128)(2,1)S(1)} %copy-done.7, bf16[128,768]{1,0:T(8,128)(2,1)S(1)} %copy-done.5), kind=kOutput, calls=%fused_computation.9 | convolution fusion | flops 253919232 | bytes 2883584 | tf_op jit(solution)/shard_map/dot_general | solution.py:105
  129.2 6.2 %psum.46 = f32[8,1,16]{2,0,1:T(8,128)} all-reduce(f32[8,1,16]{2,0,1:T(8,128)S(1)} %all_to_all.22), channel_id=1, replica_groups=mesh['grp'=4,'ep'=8] {'grp'}, use_global_device_ids=true, to_apply=%region_20.21 | all-reduce | flops 128 | bytes 1024 | tf_op jit(solution)/shard_map/psum | solution.py:155
  135.4 5.5 %all-to-all-start.3 = ((f32[8,1,16]{2,1,0:T(1,128)}), f32[8,1,16]{2,1,0:T(1,128)S(1)}, u32[]{:S(2)}, u32[]{:S(2)}) async-start(f32[8,1,16]{2,1,0:T(1,128)} %bitcast.31), calls=%async_computation.3 | async-start | bytes 8192 | tf_op jit(solution)/shard_map/all_to_all | solution.py:156
  140.9 1.6 fusion.23
  142.6 40.2 %psum.47 = f32[2,8,16]{2,1,0:T(8,128)S(1)} all-reduce(f32[2,8,16]{2,1,0:T(8,128)S(1)} %reshape.204), channel_id=1, replica_groups=mesh['grp'=4,'ep'=8] {'grp','ep'}, use_global_device_ids=true, to_apply=%region_22.23 | all-reduce | flops 256 | bytes 2048 | tf_op jit(solution)/shard_map/psum | solution.py:150
  183.0 2.0 %fusion.2 = bf16[1,768,1280]{2,1,0:T(8,128)(2,1)} fusion(bf16[128,1280]{1,0:T(8,128)(2,1)S(1)} %fusion.37, bf16[128,768]{1,0:T(8,128)(2,1)S(1)} %copy-done.6, bf16[128,768]{1,0:T(8,128)(2,1)S(1)} %copy-done.5), kind=kOutput, calls=%fused_computation.11 | convolution fusion | flops 253427712 | bytes 2686976 | tf_op jit(solution)/shard_map/dot_general | solution.py:111
  (92 shorter events, 20.4 us)
Async XLA Ops:
  7.2 61.9 %copy-start = (bf16[1,768,1280]{2,1,0:T(8,128)(2,1)S(1)}, bf16[1,768,1280]{2,1,0:T(8,128)(2,1)}, u32[]{:S(2)}) copy-start(bf16[1,768,1280]{2,1,0:T(8,128)(2,1)} %param.18) | copy-start | bytes 5898244
  7.2 6.9 %copy-start.2 = (bf16[256,1280]{1,0:T(8,128)(2,1)S(1)}, bf16[256,1280]{1,0:T(8,128)(2,1)}, u32[]{:S(2)}) copy-start(bf16[256,1280]{1,0:T(8,128)(2,1)} %param.11) | copy-start | bytes 1966084
  7.2 65.4 %all-gather.3.cloned.1.call-start = ((), (), s32[]{:S(2)}) async-start(), calls=%async_computation.4 | async-start | bytes 2211840 | tf_op jit(solution)/shard_map/all_gather | solution.py:119
  14.4 21.8 %copy-start.3 = (bf16[256,1280]{1,0:T(8,128)(2,1)S(1)}, bf16[256,1280]{1,0:T(8,128)(2,1)}, u32[]{:S(2)}) copy-start(bf16[256,1280]{1,0:T(8,128)(2,1)} %param.12) | copy-start | bytes 1966084
  19.1 13.7 %all-to-all-start.1 = ((bf16[8,1,16]{2,1,0:T(2,128)(2,1)}), bf16[8,1,16]{2,1,0:T(2,128)(2,1)S(1)}, u32[]{:S(2)}, u32[]{:S(2)}) async-start(bf16[8,1,16]{2,1,0:T(2,128)(2,1)} %all_to_all.24), calls=%async_computation.1 | async-start | bytes 8192 | tf_op jit(solution)/shard_map/all_to_all | solution.py:81
  32.8 13.6 %all-to-all-start = ((bf16[8,16,1280]{2,1,0:T(8,128)(2,1)}), bf16[8,16,1280]{2,1,0:T(8,128)(2,1)S(1)}, u32[]{:S(2)}, u32[]{:S(2)}) async-start(bf16[8,16,1280]{2,1,0:T(8,128)(2,1)} %bitcast.165), calls=%async_computation | async-start | bytes 655360 | tf_op jit(solution)/shard_map/all_to_all | solution.py:79
  46.4 22.5 %all-to-all-start.2 = ((bf16[8,16,1280]{2,1,0:T(8,128)(2,1)}), bf16[8,16,1280]{2,1,0:T(8,128)(2,1)S(1)}, u32[]{:S(2)}, u32[]{:S(2)}) async-start(bf16[8,16,1280]{2,1,0:T(8,128)(2,1)} %bitcast.166), calls=%async_computation.2 | async-start | bytes 655360 | tf_op jit(solution)/shard_map/all_to_all | solution.py:80
  50.3 61.4 %all-reduce.3.cloned.1.call-start = ((), (), s32[]{:S(2)}) async-start(), calls=%async_computation.5 | async-start | bytes 1474560 | tf_op jit(solution)/shard_map/psum | solution.py:98
  50.3 2.8 %copy-start.4 = (bf16[1,1280,768]{2,1,0:T(8,128)(2,1)S(1)}, bf16[1,1280,768]{2,1,0:T(8,128)(2,1)}, u32[]{:S(2)}) copy-start(bf16[1,1280,768]{2,1,0:T(8,128)(2,1)} %param.17) | copy-start | bytes 5898244
  74.3 1.5 copy-start.1
  74.3 1.5 copy-start.8
  74.4 1.9 copy-start.9
  75.8 1.1 copy-start.10
  121.1 3.4 %copy-start.5 = (bf16[128,768]{1,0:T(8,128)(2,1)S(1)}, bf16[128,768]{1,0:T(8,128)(2,1)}, u32[]{:S(2)}) copy-start(bf16[128,768]{1,0:T(8,128)(2,1)} %get-tuple-element.36) | copy-start | bytes 589828
  121.1 3.4 %copy-start.7 = (bf16[128,768]{1,0:T(8,128)(2,1)S(1)}, bf16[128,768]{1,0:T(8,128)(2,1)}, u32[]{:S(2)}) copy-start(bf16[128,768]{1,0:T(8,128)(2,1)} %get-tuple-element.35) | copy-start | bytes 589828
  124.5 2.0 %copy-start.6 = (bf16[128,768]{1,0:T(8,128)(2,1)S(1)}, bf16[128,768]{1,0:T(8,128)(2,1)}, u32[]{:S(2)}) copy-start(bf16[128,768]{1,0:T(8,128)(2,1)} %get-tuple-element.34) | copy-start | bytes 589828
  135.4 49.7 %all-to-all-start.3 = ((f32[8,1,16]{2,1,0:T(1,128)}), f32[8,1,16]{2,1,0:T(1,128)S(1)}, u32[]{:S(2)}, u32[]{:S(2)}) async-start(f32[8,1,16]{2,1,0:T(1,128)} %bitcast.31), calls=%async_computation.3 | async-start | bytes 8192 | tf_op jit(solution)/shard_map/all_to_all | solution.py:156
Sparse Core Ops, SparseCore 0:
  15.3 57.2 all-gather.2
  78.1 33.5 all-reduce.2
where the time goes:
time: 195 us
  waiting for transfers between devices  64.2 us (33%)
  blocking collectives  46.4 us (24%)
  matrix products  29.2 us (15%)
  starting transfers between devices  20.2 us (10%)
  between operations  14.4 us (7%)
  local copies, waits for them, and re-layouts  10.9 us (6%)
  other arithmetic  9.22 us (5%)
    psum x1, blocking collectives, body(): hot_route_all = lax.psum(hot_route_part, ('grp', 'ep'))  40.2 us
    psum x1, waiting for transfers between devices, body(): lax.psum(part_up.astype(jnp.bfloat16), 'grp').astype(jnp.float32)  33.6 us
    all_to_all x1, waiting for transfers between devices, body(): lax.all_to_all(outgoing[1], 'ep', split_axis=0, concat_axis=0, tiled=True)  14.6 us
    all_to_all x1, waiting for transfers between devices, body(): lax.all_to_all(outgoing[0], 'ep', split_axis=0, concat_axis=0, tiled=True)  9.11 us
    all_to_all x1, starting transfers between devices, body(): lax.all_to_all(outgoing[2], 'ep', split_axis=0, concat_axis=0, tiled=True)  7.28 us
    psum x1, blocking collectives, body(): cold_route = lax.psum(cold_route, 'grp')  6.24 us
    all_to_all x1, starting transfers between devices, body(): lax.all_to_all(cold_route.reshape(cold_count, capacity), 'ep', split_axis...  5.52 us
    all_to_all x1, waiting for transfers between devices, body(): lax.all_to_all(outgoing[2], 'ep', split_axis=0, concat_axis=0, tiled=True)  4.77 us
  transfers between devices with their start and end apart: 6, of which 5 were waited for; matrix products, arithmetic and copies ran while one was open for 8% of the time, Pallas kernels for 0%

commit v1 on v0

--- a/solution.py
+++ b/solution.py
@@ -147,7 +147,8 @@
     grad_gate_hot = jnp.sum(blk_gate.astype(jnp.bfloat16).astype(jnp.float32), axis=1)
     grad_up_hot = jnp.sum(blk_up.astype(jnp.bfloat16).astype(jnp.float32), axis=1)
     grad_down_hot = jnp.sum(blk_down.astype(jnp.bfloat16).astype(jnp.float32), axis=1)
-    hot_route_all = lax.psum(hot_route_part, ("grp", "ep"))
+    inner = lax.psum(hot_route_part, "ep")
+    hot_route_all = lax.psum(inner, "grp")
     me = lax.axis_index("ep")
     hot_route = lax.dynamic_index_in_dim(
         hot_route_all.reshape(hot_count, blocks, capacity), me, axis=1, keepdims=False

time: 195 us -> 183 us (0.938)
  blocking collectives: 46.4 us -> 32.1 us
  waiting for transfers between devices: 64.2 us -> 68.3 us
  starting transfers between devices: 20.2 us -> 18 us
    psum x1, blocking collectives: 40.2 us -> 21.4 us  [body(): inner = lax.psum(hot_route_part, 'ep')]
    psum x1, blocking collectives: 6.24 us -> 10.7 us  [body(): cold_route = lax.psum(cold_route, 'grp')]
    all_to_all x1, waiting for transfers between devices: 0.01 us -> 4.11 us  [body(): lax.all_to_all(cold_route.reshape(cold_count, capacity), 'ep', split_axis...]
    all_to_all x1, starting transfers between devices: 5.52 us -> 3.31 us  [body(): lax.all_to_all(cold_route.reshape(cold_count, capacity), 'ep', split_axis...]
  transfers between devices with their start and end apart: 6 -> 6, of which waited for: 5 -> 6; matrix products, arithmetic and copies ran while one was open for 8% -> 8% of each run, Pallas kernels for 0% -> 0%
where the time goes in v1:
time: 183 us; the launch traced here: 182 us
  waiting for transfers between devices  68.3 us (37%)
  blocking collectives  32.1 us (18%)
  matrix products  29.2 us (16%)
  starting transfers between devices  18 us (10%)
  between operations  14.4 us (8%)
  local copies, waits for them, and re-layouts  10.9 us (6%)
  other arithmetic  9.22 us (5%)
    psum x1, waiting for transfers between devices, body(): lax.psum(part_up.astype(jnp.bfloat16), 'grp').astype(jnp.float32)  33.6 us
    psum x1, blocking collectives, body(): inner = lax.psum(hot_route_part, 'ep')  21.4 us
    all_to_all x1, waiting for transfers between devices, body(): lax.all_to_all(outgoing[1], 'ep', split_axis=0, concat_axis=0, tiled=True)  14.6 us
    psum x1, blocking collectives, body(): cold_route = lax.psum(cold_route, 'grp')  10.7 us
    all_to_all x1, waiting for transfers between devices, body(): lax.all_to_all(outgoing[0], 'ep', split_axis=0, concat_axis=0, tiled=True)  9.11 us
    all_to_all x1, starting transfers between devices, body(): lax.all_to_all(outgoing[2], 'ep', split_axis=0, concat_axis=0, tiled=True)  7.28 us
    all_to_all x1, waiting for transfers between devices, body(): lax.all_to_all(outgoing[2], 'ep', split_axis=0, concat_axis=0, tiled=True)  4.77 us
    all_to_all x1, waiting for transfers between devices, body(): lax.all_to_all(cold_route.reshape(cold_count, capacity), 'ep', split_axis...  4.11 us
  transfers between devices with their start and end apart: 6, of which 6 were waited for; matrix products, arithmetic and copies ran while one was open for 8% of the time, Pallas kernels for 0%

profile of v1, /device:TPU:0, one launch (start us, length us, event | category | flops | bytes accessed | tf_op | source)
XLA Modules:
  0.0 182.1 jit_solution(12595181950888592070)
XLA Ops:
  15.2 2.3 %reduce-window.14 = s32[8,12,128]{2,1,0:T(8,128)S(1)} reduce-window(s32[8,12,128]{2,1,0:T(8,128)S(1)} %fusion.69, s32[]{:T(128)} %constant.15.clone.1), window={size=1x1x128 pad=0_0x0_0x127_0}, to_apply=%region_1.2 | reduce-window | flops 1560576 | bytes 98308 | tf_op jit(solution)/shard_map/reduce-window
  19.1 7.3 %all-to-all-start.1 = ((bf16[8,1,16]{2,1,0:T(2,128)(2,1)}), bf16[8,1,16]{2,1,0:T(2,128)(2,1)S(1)}, u32[]{:S(2)}, u32[]{:S(2)}) async-start(bf16[8,1,16]{2,1,0:T(2,128)(2,1)} %all_to_all.24), calls=%async_computation.1 | async-start | bytes 8192 | tf_op jit(solution)/shard_map/all_to_all | solution.py:81
  28.0 4.8 %all-to-all-done.1 = bf16[8,1,16]{2,1,0:T(2,128)(2,1)S(1)} async-done(((bf16[8,1,16]{2,1,0:T(2,128)(2,1)}), bf16[8,1,16]{2,1,0:T(2,128)(2,1)S(1)}, u32[]{:S(2)}, u32[]{:S(2)}) %all-to-all-start.1) | async-done | bytes 288 | tf_op jit(solution)/shard_map/all_to_all | solution.py:81
  32.8 3.4 %all-to-all-start = ((bf16[8,16,1280]{2,1,0:T(8,128)(2,1)}), bf16[8,16,1280]{2,1,0:T(8,128)(2,1)S(1)}, u32[]{:S(2)}, u32[]{:S(2)}) async-start(bf16[8,16,1280]{2,1,0:T(8,128)(2,1)} %bitcast.165), calls=%async_computation | async-start | bytes 655360 | tf_op jit(solution)/shard_map/all_to_all | solution.py:79
  37.3 9.1 %all-to-all-done = bf16[8,16,1280]{2,1,0:T(8,128)(2,1)S(1)} async-done(((bf16[8,16,1280]{2,1,0:T(8,128)(2,1)}), bf16[8,16,1280]{2,1,0:T(8,128)(2,1)S(1)}, u32[]{:S(2)}, u32[]{:S(2)}) %all-to-all-start) | async-done | bytes 327712 | tf_op jit(solution)/shard_map/all_to_all | solution.py:79
  46.4 3.9 %all-to-all-start.2 = ((bf16[8,16,1280]{2,1,0:T(8,128)(2,1)}), bf16[8,16,1280]{2,1,0:T(8,128)(2,1)S(1)}, u32[]{:S(2)}, u32[]{:S(2)}) async-start(bf16[8,16,1280]{2,1,0:T(8,128)(2,1)} %bitcast.166), calls=%async_computation.2 | async-start | bytes 655360 | tf_op jit(solution)/shard_map/all_to_all | solution.py:80
  50.3 2.8 %fusion.20 = bf16[128,768]{1,0:T(8,128)(2,1)} fusion(bf16[128,1280]{1,0:T(8,128)(2,1)S(1)} %bitcast.155, bf16[1,1280,768]{2,1,0:T(8,128)(2,1)} %param.16), kind=kOutput, calls=%fused_computation.29 | convolution fusion | flops 251756544 | bytes 2490368 | tf_op jit(solution)/shard_map/dot_general | solution.py:91
  54.3 14.6 %all-to-all-done.2 = bf16[8,16,1280]{2,1,0:T(8,128)(2,1)S(1)} async-done(((bf16[8,16,1280]{2,1,0:T(8,128)(2,1)}), bf16[8,16,1280]{2,1,0:T(8,128)(2,1)S(1)}, u32[]{:S(2)}, u32[]{:S(2)}) %all-to-all-start.2) | async-done | bytes 327712 | tf_op jit(solution)/shard_map/all_to_all | solution.py:80
  69.0 1.5 fusion.14
  70.5 2.1 %all-gather.3.cloned.1.call-done = bf16[3,256,1280]{2,1,0:T(8,128)(2,1)} async-done(((bf16[3,32,1280]{2,1,0:T(8,128)(2,1)}), bf16[3,256,1280]{2,1,0:T(8,128)(2,1)}) %all-gather.3.cloned.1.call-update) | async-done | bytes 1966096 | tf_op jit(solution)/shard_map/all_gather | solution.py:119
  72.6 1.7 copy.68
  78.1 33.6 %all-reduce.4.cloned.1.call-done = (bf16[128,768]{1,0:T(8,128)(2,1)}, bf16[128,768]{1,0:T(8,128)(2,1)}, bf16[128,768]{1,0:T(8,128)(2,1)}, bf16[3,2,128,96]{2,3,1,0:T(8,128)(2,1)}) async-done(((bf16[128,768]{1,0:T(8,128)(2,1)}, bf16[128,768]{1,0:T(8,128)(2,1)}, bf16[128,768]{1,0:T(8,128)(2,1)}, bf16[3,2,128,96]{2,3,1,0:T(8,128)(2,1)}), (bf16[128,768]{1,0:T(8,128)(2,1)}, bf16[128,768]{1,0:T(8,128)(2,1)}, ...) | async-done | bytes 737296 | tf_op jit(solution)/shard_map/psum | solution.py:98
  111.7 1.6 convert_element_type.217
  114.5 3.3 %convert_reduce_fusion = f32[2,96,1280]{2,1,0:T(8,128)} fusion(f32[2,8,16,96]{3,2,1,0:T(8,128)S(1)} %bitcast.169, f32[2,8,16,96]{3,2,1,0:T(8,128)S(1)} %bitcast.171, bf16[3,2,8,16,1280]{4,3,2,1,0:T(8,128)(2,1)} %bitcast.152), kind=kOutput, calls=%fused_computation | convolution fusion | flops 68714496 | bytes 1835008 | tf_op jit(solution)/shard_map/jbch,jbcd->jbhd/dot_general | solution.py:146
  117.8 3.3 %convert_reduce_fusion.2 = f32[2,1280,96]{1,2,0:T(8,128)} fusion(f32[2,8,16,96]{3,2,1,0:T(8,128)S(1)} %bitcast.172, f32[2,8,16,96]{3,2,1,0:T(8,128)S(1)} %bitcast.174, f32[2,8,16,96]{3,2,1,0:T(8,128)S(1)} %bitcast.170, bf16[3,2,8,16,1280]{4,3,2,1,0:T(8,128)(2,1)} %bitcast.153), kind=kOutput, calls=%fused_computation.2 | convolution fusion | flops 68812800 | bytes 1933312 | tf_op jit(solution)/shard_map/jbcd,jbch->jbdh/dot_general | solution.py:144
  121.1 3.4 %convert_reduce_fusion.1 = f32[2,1280,96]{1,2,0:T(8,128)} fusion(f32[2,8,16,96]{3,2,1,0:T(8,128)S(1)} %bitcast.175, f32[2,8,16,96]{3,2,1,0:T(8,128)S(1)} %bitcast.173, bf16[3,2,8,16,1280]{4,3,2,1,0:T(8,128)(2,1)} %bitcast.154), kind=kOutput, calls=%fused_computation.1 | convolution fusion | flops 68714496 | bytes 1835008 | tf_op jit(solution)/shard_map/jbcd,jbch->jbdh/dot_general | solution.py:145
  124.6 2.0 %fusion.1 = bf16[1,1280,768]{2,1,0:T(8,128)(2,1)} fusion(bf16[128,1280]{1,0:T(8,128)(2,1)S(1)} %bitcast.157, bf16[128,768]{1,0:T(8,128)(2,1)S(1)} %copy-done.7, bf16[128,768]{1,0:T(8,128)(2,1)S(1)} %copy-done.5), kind=kOutput, calls=%fused_computation.10 | convolution fusion | flops 253427712 | bytes 2686976 | tf_op jit(solution)/shard_map/dot_general | solution.py:108
  126.5 2.0 %fusion = bf16[1,1280,768]{2,1,0:T(8,128)(2,1)} fusion(bf16[128,1280]{1,0:T(8,128)(2,1)S(1)} %bitcast.158, bf16[128,768]{1,0:T(8,128)(2,1)S(1)} %copy-done.6, bf16[128,768]{1,0:T(8,128)(2,1)S(1)} %copy-done.7, bf16[128,768]{1,0:T(8,128)(2,1)S(1)} %copy-done.5), kind=kOutput, calls=%fused_computation.9 | convolution fusion | flops 253919232 | bytes 2883584 | tf_op jit(solution)/shard_map/dot_general | solution.py:105
  129.2 1.6 fusion.23
  130.8 21.4 %psum.54 = f32[2,128]{1,0:T(2,128)S(1)} all-reduce(f32[2,128]{1,0:T(2,128)S(1)} %fusion.23), channel_id=1, replica_groups=mesh['grp'=4,'ep'=8] {'ep'}, use_global_device_ids=true, to_apply=%region_22.23 | all-reduce | flops 256 | bytes 2048 | tf_op jit(solution)/shard_map/psum | solution.py:150
  152.3 10.7 %all-reduce = (f32[8,1,16]{2,0,1:T(8,128)}, f32[2,8,16]{2,1,0:T(8,128)S(1)}) all-reduce(f32[8,1,16]{2,0,1:T(8,128)S(1)} %all_to_all.22, f32[2,8,16]{2,1,0:T(8,128)S(1)} %reshape.204), channel_id=1, replica_groups=mesh['grp'=4,'ep'=8] {'grp'}, use_global_device_ids=true, to_apply=%region_20.21 | all-reduce | flops 384 | bytes 3072 | tf_op jit(solution)/shard_map/psum | solution.py:156
  163.1 3.3 %all-to-all-start.3 = ((f32[8,1,16]{2,1,0:T(1,128)}), f32[8,1,16]{2,1,0:T(1,128)S(1)}, u32[]{:S(2)}, u32[]{:S(2)}) async-start(f32[8,1,16]{2,1,0:T(1,128)} %bitcast.31), calls=%async_computation.3 | async-start | bytes 8192 | tf_op jit(solution)/shard_map/all_to_all | solution.py:157
  166.4 2.0 %fusion.2 = bf16[1,768,1280]{2,1,0:T(8,128)(2,1)} fusion(bf16[128,1280]{1,0:T(8,128)(2,1)S(1)} %fusion.37, bf16[128,768]{1,0:T(8,128)(2,1)S(1)} %copy-done.6, bf16[128,768]{1,0:T(8,128)(2,1)S(1)} %copy-done.5), kind=kOutput, calls=%fused_computation.11 | convolution fusion | flops 253427712 | bytes 2686976 | tf_op jit(solution)/shard_map/dot_general | solution.py:111
  168.6 4.1 %all-to-all-done.3 = f32[8,1,16]{2,1,0:T(1,128)S(1)} async-done(((f32[8,1,16]{2,1,0:T(1,128)}), f32[8,1,16]{2,1,0:T(1,128)S(1)}, u32[]{:S(2)}, u32[]{:S(2)}) %all-to-all-start.3) | async-done | bytes 544 | tf_op jit(solution)/shard_map/all_to_all | solution.py:157
  (92 shorter events, 21.8 us)
Async XLA Ops:
  7.2 61.9 %copy-start = (bf16[1,768,1280]{2,1,0:T(8,128)(2,1)S(1)}, bf16[1,768,1280]{2,1,0:T(8,128)(2,1)}, u32[]{:S(2)}) copy-start(bf16[1,768,1280]{2,1,0:T(8,128)(2,1)} %param.18) | copy-start | bytes 5898244
  7.2 6.9 %copy-start.2 = (bf16[256,1280]{1,0:T(8,128)(2,1)S(1)}, bf16[256,1280]{1,0:T(8,128)(2,1)}, u32[]{:S(2)}) copy-start(bf16[256,1280]{1,0:T(8,128)(2,1)} %param.11) | copy-start | bytes 1966084
  7.2 65.4 %all-gather.3.cloned.1.call-start = ((), (), s32[]{:S(2)}) async-start(), calls=%async_computation.4 | async-start | bytes 2211840 | tf_op jit(solution)/shard_map/all_gather | solution.py:119
  14.4 21.8 %copy-start.3 = (bf16[256,1280]{1,0:T(8,128)(2,1)S(1)}, bf16[256,1280]{1,0:T(8,128)(2,1)}, u32[]{:S(2)}) copy-start(bf16[256,1280]{1,0:T(8,128)(2,1)} %param.12) | copy-start | bytes 1966084
  19.1 13.7 %all-to-all-start.1 = ((bf16[8,1,16]{2,1,0:T(2,128)(2,1)}), bf16[8,1,16]{2,1,0:T(2,128)(2,1)S(1)}, u32[]{:S(2)}, u32[]{:S(2)}) async-start(bf16[8,1,16]{2,1,0:T(2,128)(2,1)} %all_to_all.24), calls=%async_computation.1 | async-start | bytes 8192 | tf_op jit(solution)/shard_map/all_to_all | solution.py:81
  32.8 13.6 %all-to-all-start = ((bf16[8,16,1280]{2,1,0:T(8,128)(2,1)}), bf16[8,16,1280]{2,1,0:T(8,128)(2,1)S(1)}, u32[]{:S(2)}, u32[]{:S(2)}) async-start(bf16[8,16,1280]{2,1,0:T(8,128)(2,1)} %bitcast.165), calls=%async_computation | async-start | bytes 655360 | tf_op jit(solution)/shard_map/all_to_all | solution.py:79
  46.4 22.5 %all-to-all-start.2 = ((bf16[8,16,1280]{2,1,0:T(8,128)(2,1)}), bf16[8,16,1280]{2,1,0:T(8,128)(2,1)S(1)}, u32[]{:S(2)}, u32[]{:S(2)}) async-start(bf16[8,16,1280]{2,1,0:T(8,128)(2,1)} %bitcast.166), calls=%async_computation.2 | async-start | bytes 655360 | tf_op jit(solution)/shard_map/all_to_all | solution.py:80
  50.3 61.4 %all-reduce.4.cloned.1.call-start = ((), (), s32[]{:S(2)}) async-start(), calls=%async_computation.5 | async-start | bytes 1474560 | tf_op jit(solution)/shard_map/psum | solution.py:98
  50.3 2.8 %copy-start.4 = (bf16[1,1280,768]{2,1,0:T(8,128)(2,1)S(1)}, bf16[1,1280,768]{2,1,0:T(8,128)(2,1)}, u32[]{:S(2)}) copy-start(bf16[1,1280,768]{2,1,0:T(8,128)(2,1)} %param.17) | copy-start | bytes 5898244
  74.3 1.5 copy-start.1
  74.3 1.5 copy-start.8
  74.4 1.9 %copy-start.9 = (bf16[2,1280,96]{1,2,0:T(8,128)(2,1)S(1)}, bf16[2,1280,96]{1,2,0:T(8,128)(2,1)}, u32[]{:S(2)}) copy-start(bf16[2,1280,96]{1,2,0:T(8,128)(2,1)} %param.19) | copy-start | bytes 1474564
  75.8 1.1 copy-start.10
  121.1 3.4 %copy-start.5 = (bf16[128,768]{1,0:T(8,128)(2,1)S(1)}, bf16[128,768]{1,0:T(8,128)(2,1)}, u32[]{:S(2)}) copy-start(bf16[128,768]{1,0:T(8,128)(2,1)} %get-tuple-element.38) | copy-start | bytes 589828
  121.1 3.4 %copy-start.7 = (bf16[128,768]{1,0:T(8,128)(2,1)S(1)}, bf16[128,768]{1,0:T(8,128)(2,1)}, u32[]{:S(2)}) copy-start(bf16[128,768]{1,0:T(8,128)(2,1)} %get-tuple-element.37) | copy-start | bytes 589828
  124.5 2.0 %copy-start.6 = (bf16[128,768]{1,0:T(8,128)(2,1)S(1)}, bf16[128,768]{1,0:T(8,128)(2,1)}, u32[]{:S(2)}) copy-start(bf16[128,768]{1,0:T(8,128)(2,1)} %get-tuple-element.36) | copy-start | bytes 589828
  163.1 9.6 %all-to-all-start.3 = ((f32[8,1,16]{2,1,0:T(1,128)}), f32[8,1,16]{2,1,0:T(1,128)S(1)}, u32[]{:S(2)}, u32[]{:S(2)}) async-start(f32[8,1,16]{2,1,0:T(1,128)} %bitcast.31), calls=%async_computation.3 | async-start | bytes 8192 | tf_op jit(solution)/shard_map/all_to_all | solution.py:157
Sparse Core Ops, SparseCore 0:
  15.3 57.2 all-gather.2
  78.1 33.5 all-reduce.3
